TPU v7x, 256 devices: a whole 4x4x8 slice. The times are simulated.
256 devices in a mesh: dp: 8 (over z), seq: 32 (over y, x, core).
Axes of the slice: x: 4, y: 4, z: 8, core: 2. Of those that a mesh axis runs over, the one named last changes fastest.
Arguments:
- inputs: bfloat16 [8, 4096, 2048], P('dp', 'seq'), may hold values from -6 to 6
- weight_codes: bfloat16 [2048, 1280], P('seq'), may hold values from -4 to 4
- scales: bfloat16 [2048, 10], P('seq'), may hold values from 0.010986328 to 0.043945312
- log_decay: float32 [8, 16, 4096], P('dp', None, 'seq'), may hold values from -0.85 to 0, as said below
- cotangent: bfloat16 [8, 4096, 1024], P('dp', 'seq'), may hold values from -6 to 6
Outputs:
- grad_inputs: float32 [8, 4096, 2048], P('dp', 'seq')
- grad_weight: float32 [2048, 1280], P('seq')
Inputs may be any that keep to these rules, and one draw needn't show every extreme that they name: log_decay is negative everywhere.
All inputs are finite; a program needn't handle non-finite values.
Results may differ from a plain program's by a relative error of at most 0.017.
Values may be sent and summed in bfloat16 or wider, within the bound.
No kernel may reach another device: no remote copies, remote signals or barrier semaphores. Data moves between devices by JAX's collectives and lax.ppermute only.
A program may use at most 128 MiB of HBM per device.

v0:
```python
import math
import jax
import jax.numpy as jnp
from jax import lax
from jax.sharding import PartitionSpec as P


def entering(part, axis, combine, identity, reverse):
    count = lax.axis_size(axis)
    place = lax.axis_index(axis)
    ahead = count - 1 - place if reverse else place
    gathered = jax.tree.map(lambda a: lax.all_gather(a, axis), part)
    state = jax.tree.map(lambda a, e: jnp.zeros_like(a) + jnp.asarray(e, a.dtype), part, identity)

    def one(hop, state):
        source = count - 1 - hop if reverse else hop
        return combine(
            state, jax.tree.map(lambda a: lax.dynamic_index_in_dim(a, source, 0, False), gathered)
        )

    return lax.fori_loop(0, ahead, one, state)


def dequantize(code_rows, scale_rows):
    row_count, col_count = code_rows.shape
    group_count = scale_rows.shape[1]
    spread = code_rows.astype(jnp.float32).reshape(row_count, group_count, col_count // group_count)
    spread = spread * scale_rows.astype(jnp.float32)[:, :, None]
    return spread.reshape(row_count, col_count).astype(jnp.bfloat16)


def block_prep(ld_block):
    cum_log = jnp.cumsum(ld_block, axis=1)
    input_scale = jnp.sqrt(-jnp.expm1(2.0 * ld_block))
    tail_weight = jnp.exp(cum_log[:, -1:] - cum_log) * input_scale
    return (cum_log, input_scale, tail_weight)


def weighted_pair(x_vals, grad_out, tail_weight, cum_log, inv_root):
    head_weight = jnp.exp(cum_log) * inv_root
    weighted_x = (x_vals.astype(jnp.float32) * tail_weight.T[:, :, None]).astype(jnp.bfloat16)
    weighted_g = (grad_out.astype(jnp.float32) * head_weight.T[:, :, None]).astype(jnp.bfloat16)
    return (weighted_x, weighted_g)


def summaries(x_vals, b_mat, c_mat, grad_out, ld_block):
    cum_log, input_scale, tail_weight = block_prep(ld_block)
    inv_root = 1.0 / math.sqrt(b_mat.shape[1])
    weighted_x, weighted_g = weighted_pair(x_vals, grad_out, tail_weight, cum_log, inv_root)
    fwd_state = jnp.einsum("sn,shp->hnp", b_mat, weighted_x, preferred_element_type=jnp.float32)
    back_state = jnp.einsum("tn,thp->hnp", c_mat, weighted_g, preferred_element_type=jnp.float32)
    return (jnp.exp(cum_log[:, -1]), fwd_state, back_state)


def block_grads(x_vals, b_mat, c_mat, grad_out, ld_block, state_in, back_in):
    block_len = ld_block.shape[1]
    cum_log, input_scale, tail_weight = block_prep(ld_block)
    inv_root = 1.0 / math.sqrt(b_mat.shape[1])
    weighted_x, weighted_g = weighted_pair(x_vals, grad_out, tail_weight, cum_log, inv_root)
    row_ids = lax.broadcasted_iota(jnp.int32, (block_len, block_len), 0)
    col_ids = lax.broadcasted_iota(jnp.int32, (block_len, block_len), 1)
    lower_mask = (row_ids >= col_ids)[None]
    log_gap = cum_log[:, :, None] - cum_log[:, None, :]
    decay_mat = jnp.where(lower_mask, jnp.exp(jnp.where(lower_mask, log_gap, 0.0)), 0.0)
    state_low = state_in.astype(jnp.bfloat16)
    back_low = back_in.astype(jnp.bfloat16)
    x_dot_g = jnp.einsum("thp,shp->hts", grad_out, x_vals, preferred_element_type=jnp.float32)
    c_dot_b = jnp.dot(c_mat, b_mat.T, preferred_element_type=jnp.float32)
    mix_weights = (
        jnp.sum(decay_mat * input_scale[:, None, :] * x_dot_g, axis=0) * inv_root
    ).astype(jnp.bfloat16)
    d_c = jnp.einsum("hnp,thp->tn", state_low, weighted_g, preferred_element_type=jnp.float32)
    d_c = d_c + jnp.dot(mix_weights, b_mat, preferred_element_type=jnp.float32)
    d_b = jnp.einsum("hnp,thp->tn", back_low, weighted_x, preferred_element_type=jnp.float32)
    d_b = d_b + jnp.dot(mix_weights.T, c_mat, preferred_element_type=jnp.float32)
    d_x = (
        jnp.einsum("tn,hnp->thp", b_mat, back_low, preferred_element_type=jnp.float32)
        * tail_weight.T[:, :, None]
    )
    inner_weights = (decay_mat * c_dot_b[None] * inv_root).astype(jnp.bfloat16)
    inner = jnp.einsum("hus,uhp->shp", inner_weights, grad_out, preferred_element_type=jnp.float32)
    d_x = d_x + input_scale.T[:, :, None] * inner
    return (d_x, d_b, d_c)


def state_chain(decays, adds, start, backward):

    def step(carry, item):
        return (item[0][:, None, None] * carry + item[1], carry)

    return lax.scan(step, start, (decays, adds), reverse=backward)


def join_summary(earlier, later):
    return (earlier[0] * later[0], later[0][:, None, None] * earlier[1] + later[1])


def local(inputs, weight_codes, scales, log_decay, cotangent):
    tok_count = inputs.shape[1]
    features = inputs[0]
    grad_out = cotangent[0]
    head_count = log_decay.shape[1]
    hp_width = grad_out.shape[1]
    head_dim = hp_width // head_count
    proj_width = weight_codes.shape[1]
    state_width = (proj_width - hp_width) // 2
    full_codes, full_scales = (
        lax.all_gather(weight_codes, "seq", axis=0, tiled=True),
        lax.all_gather(scales, "seq", axis=0, tiled=True),
    )
    weights = dequantize(full_codes, full_scales)
    projected = jnp.dot(features, weights, preferred_element_type=jnp.float32).astype(jnp.bfloat16)
    block_len = min(128, tok_count)
    block_count = tok_count // block_len
    x_blocks = projected[:, :hp_width].reshape(block_count, block_len, head_count, head_dim)
    b_blocks = projected[:, hp_width : hp_width + state_width].reshape(
        block_count, block_len, state_width
    )
    c_blocks = projected[:, hp_width + state_width :].reshape(block_count, block_len, state_width)
    g_blocks = grad_out.reshape(block_count, block_len, head_count, head_dim)
    ld_blocks = log_decay[0].reshape(head_count, block_count, block_len).transpose(1, 0, 2)
    decays, fwd_states, back_states = jax.vmap(summaries)(
        x_blocks, b_blocks, c_blocks, g_blocks, ld_blocks
    )
    zero_state = jnp.zeros((head_count, state_width, head_dim), jnp.float32)
    dev_decay = jnp.prod(decays, axis=0)
    dev_fwd, unused_a = state_chain(decays, fwd_states, zero_state, False)
    dev_back, unused_b = state_chain(decays, back_states, zero_state, True)
    neutral = (jnp.ones((head_count,), jnp.float32), zero_state)
    carried = entering((dev_decay, dev_fwd), "seq", join_summary, neutral, False)
    returned = entering((dev_decay, dev_back), "seq", join_summary, neutral, True)
    unused_c, state_starts = state_chain(decays, fwd_states, carried[1], False)
    unused_d, back_starts = state_chain(decays, back_states, returned[1], True)
    d_x, d_b, d_c = lax.map(
        lambda block_item: block_grads(*block_item),
        (x_blocks, b_blocks, c_blocks, g_blocks, ld_blocks, state_starts, back_starts),
    )
    d_proj = jnp.concatenate(
        [
            d_x.reshape(tok_count, hp_width),
            d_b.reshape(tok_count, state_width),
            d_c.reshape(tok_count, state_width),
        ],
        axis=1,
    ).astype(jnp.bfloat16)
    grad_in = lax.dot_general(
        d_proj, weights, (((1,), (1,)), ((), ())), preferred_element_type=jnp.float32
    )
    seq_count = lax.axis_size("seq")
    group_count = lax.axis_size("dp")
    norm_factor = 1.0 / math.sqrt(group_count * seq_count * tok_count)
    partial_grad = lax.psum_scatter(
        lax.dot_general(
            features, d_proj, (((0,), (0,)), ((), ())), preferred_element_type=jnp.float32
        ),
        "seq",
        scatter_dimension=0,
        tiled=True,
    )
    summed_grad = lax.psum(partial_grad, "dp")
    return (grad_in[None], summed_grad * norm_factor)


def solution(mesh):
    placed = (
        P("dp", "seq", None),
        P("seq", None),
        P("seq", None),
        P("dp", None, "seq"),
        P("dp", "seq", None),
    )
    return jax.shard_map(
        local,
        mesh=mesh,
        in_specs=placed,
        out_specs=(P("dp", "seq", None), P("seq", None)),
        check_vma=False,
    )
```

profile of v0, /device:TPU:2, one launch (start us, length us, event | category | flops | bytes accessed | tf_op | source)
XLA Modules:
  0.0 521.6 jit_solution(17085878530613788069)
XLA Ops:
  8.0 24.6 %all-gather.1 = bf16[32,64,10]{1,2,0:T(8,128)(2,1)S(1)} all-gather(bf16[1,64,10]{1,2,0:T(8,128)(2,1)} %bitcast.145), channel_id=1, replica_groups=mesh['dp'=8,'seq'=32] {'seq'}, dimensions={0}, use_global_device_ids=true | all-gather | bytes 42240 | tf_op jit(solution)/shard_map/all_gather | solution.py:109
  35.8 1.3 fusion.43
  37.1 28.6 %all-gather.6.cloned.1.call-done = bf16[2048,1280]{1,0:T(8,128)(2,1)} async-done(((bf16[64,1280]{1,0:T(8,128)(2,1)}), bf16[2048,1280]{1,0:T(8,128)(2,1)}) %all-gather.6.cloned.1.call-update) | async-done | bytes 5242896 | tf_op jit(solution)/shard_map/all_gather | solution.py:108
  65.7 7.9 %copy.59 = bf16[2048,1280]{0,1:T(8,128)(2,1)} copy(bf16[2048,1280]{1,0:T(8,128)(2,1)} %all-gather.6.cloned.1.call-done) | data formatting | bytes 10485760 | tf_op jit(solution)/shard_map/all_gather | solution.py:108
  73.6 3.9 fusion
  77.6 2.4 copy-done.2
  80.0 1.5 fusion.1
  85.5 21.4 %all-gather = f32[32,16,1]{1,2,0:T(1,128)} all-gather(f32[1,16,1]{1,2,0:T(1,128)S(1)} %exp.58), channel_id=2, replica_groups=mesh['dp'=8,'seq'=32] {'seq'}, dimensions={0}, use_global_device_ids=true | all-gather | bytes 2112 | tf_op jit(solution)/shard_map/all_gather | solution.py:12
  108.7 52.1 %all-gather.10.cloned.1.call-done = f32[32,16,128,64]{2,3,1,0:T(8,128)} async-done(((f32[1,16,128,64]{2,3,1,0:T(8,128)}), f32[32,16,128,64]{2,3,1,0:T(8,128)}) %all-gather.10.cloned.1.call-update) | async-done | bytes 16777232 | tf_op jit(solution)/shard_map/all_gather | solution.py:12
  160.9 4.7 while.17
  160.9 1.1 constant_dynamic-slice_fusion.5
  163.3 1.1 constant_dynamic-slice_fusion.5
  165.6 74.8 %all-gather.8.cloned.1.call-done = f32[32,16,128,64]{2,3,1,0:T(8,128)} async-done(((f32[1,16,128,64]{2,3,1,0:T(8,128)}), f32[32,16,128,64]{2,3,1,0:T(8,128)}) %all-gather.8.cloned.1.call-update) | async-done | bytes 16777232 | tf_op jit(solution)/shard_map/all_gather | solution.py:12
  240.5 68.7 %while.16 = (s32[]{:T(128)}, f32[16,128,64]{2,1,0:T(8,128)S(1)}, s32[]{:T(128)}, f32[32,16]{1,0:T(8,128)}, f32[32,16,128,64]{2,3,1,0:T(8,128)}, /*index=5*/s32[]{:T(128)}, s32[]{:T(128)}, s32[]{:T(128)}, s32[]{:T(128)}) while((s32[]{:T(128)}, f32[16,128,64]{2,1,0:T(8,128)S(1)}, s32[]{:T(128)}, f32[32,16]{1,0:T(8,128)}, ...), condition=%wide.region_2.3_spmd, body=%wide.region_1.2_spmd.sunk | while | flops 262150 | bytes 3670363 | solution.py:21
  245.3 1.1 constant_dynamic-slice_fusion.4
  309.6 1.2 convolution_bitcast_fusion.7
  310.8 1.5 convolution_bitcast_fusion.6
  313.5 5.3 %convolution_bitcast_fusion = f32[2048,1280]{0,1:T(8,128)} fusion(bf16[1,128,2048]{2,1,0:T(8,128)(2,1)S(1)} %copy-done, bf16[128,128]{0,1:T(8,128)(2,1)S(1)} %fusion.12, bf16[128,128]{0,1:T(8,128)(2,1)S(1)} %fusion.11, bf16[128,1024]{0,1:T(8,128)(2,1)S(1)} %bitcast.132), kind=kOutput, calls=%fused_computation.8 | convolution fusion | flops 672071680 | bytes 11337728 | tf_op jit(solution)/shard_map/dot_general | solution.py:153
  318.9 11.3 %copy.89 = f32[2048,1280]{1,0:T(8,128)} copy(f32[2048,1280]{0,1:T(8,128)} %convolution_bitcast_fusion) | data formatting | bytes 20971520
  330.2 106.7 %reduce-scatter.4.cloned.1.call-done = f32[64,1280]{1,0:T(8,128)} async-done(((f32[2048,1280]{1,0:T(8,128)}), f32[64,1280]{1,0:T(8,128)}) %reduce-scatter.4.cloned.1.call-update) | async-done | bytes 327696
  436.9 2.1 copy.90
  439.0 4.3 convolution_bitcast_fusion.1
  443.4 69.7 %all-reduce.2.cloned.1.call-done = f32[64,1280]{0,1:T(8,128)} async-done(((f32[64,1280]{0,1:T(8,128)}), f32[64,1280]{0,1:T(8,128)}) %all-reduce.2.cloned.1.call-update) | async-done | bytes 327696 | tf_op jit(solution)/shard_map/psum | solution.py:160
  513.0 1.1 broadcast_multiply_fusion
  (178 shorter events, 81.2 us)
Async XLA Ops:
  7.2 72.8 %copy-start = (bf16[1,128,2048]{2,1,0:T(8,128)(2,1)S(1)}, bf16[1,128,2048]{2,1,0:T(8,128)(2,1)}, u32[]{:S(2)}) copy-start(bf16[1,128,2048]{2,1,0:T(8,128)(2,1)} %param.9) | copy-start | bytes 1572868
  7.2 58.5 %all-gather.6.cloned.1.call-start = ((), (), s32[]{:S(2)}) async-start(), calls=%async_computation.1 | async-start | bytes 5406720 | tf_op jit(solution)/shard_map/all_gather | solution.py:108
  7.9 152.9 %all-gather.10.cloned.1.call-start = ((), (), s32[]{:S(2)}) async-start(), calls=%async_computation.3 | async-start | bytes 17301504 | tf_op jit(solution)/shard_map/all_gather | solution.py:12
  77.6 2.4 copy-start.2
  79.9 3.4 copy-start.5
  83.3 157.1 %all-gather.8.cloned.1.call-start = ((), (), s32[]{:S(2)}) async-start(), calls=%async_computation.2 | async-start | bytes 17301504 | tf_op jit(solution)/shard_map/all_gather | solution.py:12
  83.6 77.2 %copy-start.3 = (bf16[1,128,1024]{1,2,0:T(8,128)(2,1)}, bf16[1,128,1024]{1,2,0:T(8,128)(2,1)S(1)}, u32[]{:S(2)}) copy-start(bf16[1,128,1024]{1,2,0:T(8,128)(2,1)S(1)} %copy.63) | copy-start | bytes 786436
  85.4 351.5 %reduce-scatter.4.cloned.1.call-start = ((), (), s32[]{:S(2)}) async-start(), calls=%async_computation.5 | async-start | bytes 10813440
  106.9 53.9 %copy-start.7 = (pred[128,128]{0,1:T(8,128)(4,1)}, pred[128,128]{0,1:T(8,128)(4,1)S(1)}, u32[]{:S(2)}) copy-start(pred[128,128]{0,1:T(8,128)(4,1)S(1)} %iota_compare_fusion) | copy-start | bytes 49156
  165.6 74.9 %copy-start.1 = (f32[16,128,64]{2,1,0:T(8,128)}, f32[16,128,64]{2,1,0:T(8,128)S(1)}, u32[]{:S(2)}) copy-start(f32[16,128,64]{2,1,0:T(8,128)S(1)} %get-tuple-element.218) | copy-start | bytes 1572868
  309.2 3.7 copy-start.4
  309.2 3.7 copy-start.6
  309.2 3.7 copy-start.8
  309.3 3.7 copy-start.9
  330.2 182.8 %all-reduce.2.cloned.1.call-start = ((), (), s32[]{:S(2)}) async-start(), calls=%async_computation.4 | async-start | bytes 1310720 | tf_op jit(solution)/shard_map/psum | solution.py:160
Sparse Core Ops, SparseCore 0:
  10.6 55.0 all-gather.5
  83.4 77.2 all-gather.9
  163.3 77.0 all-gather.7
  330.3 106.5 reduce-scatter.3
  439.2 73.7 all-reduce.1
where the time goes:
time: 525 us; the launch traced here: 522 us
  waiting for transfers between devices  333 us (63%)
  local copies, waits for them, and re-layouts  91.1 us (17%)
  blocking collectives  46 us (9%)
  matrix products  18.9 us (4%)
  other arithmetic  17.6 us (3%)
  between operations  14 us (3%)
    all_gather x2, waiting for transfers between devices, entering(): gathered = jax.tree.map(lambda a: lax.all_gather(a, axis), part)  127 us
    unnamed x6, waiting for transfers between devices  107 us
    psum x1, waiting for transfers between devices, local(): summed_grad = lax.psum(partial_grad, 'dp')  69.7 us
    dynamic_slice x62, local copies, waits for them, and re-layouts, one(): lax.dynamic_index_in_dim(a, source, 0, False)  43.9 us
    all_gather x1, waiting for transfers between devices, local(): lax.all_gather(weight_codes, 'seq', axis=0, tiled=True)  28.6 us
    all_gather x1, blocking collectives, local(): lax.all_gather(scales, 'seq', axis=0, tiled=True)  24.6 us
    mul x31, local copies, waits for them, and re-layouts, join_summary(): later[0][:, None, None] * earlier[1] + later[1]  21.4 us
    all_gather x1, blocking collectives, entering(): gathered = jax.tree.map(lambda a: lax.all_gather(a, axis), part)  21.4 us
  transfers between devices with their start and end apart: 5, of which 5 were waited for; matrix products, arithmetic and copies ran while one was open for 3% of the time, Pallas kernels for 0%

commit v1 on v0

--- a/solution.py
+++ b/solution.py
@@ -3,6 +3,11 @@
 import jax.numpy as jnp
 from jax import lax
 from jax.sharding import PartitionSpec as P
+
+
+def gather_by_exchange(x, axis, dim):
+    copies = jnp.concatenate([x] * lax.axis_size(axis), axis=dim)
+    return lax.all_to_all(copies, axis, dim, dim, tiled=True)
 
 
 def entering(part, axis, combine, identity, reverse):
@@ -105,7 +110,7 @@
     proj_width = weight_codes.shape[1]
     state_width = (proj_width - hp_width) // 2
     full_codes, full_scales = (
-        lax.all_gather(weight_codes, "seq", axis=0, tiled=True),
+        gather_by_exchange(weight_codes, "seq", 0),
         lax.all_gather(scales, "seq", axis=0, tiled=True),
     )
     weights = dequantize(full_codes, full_scales)

time: 525 us -> 604 us (1.15)
  waiting for transfers between devices: 333 us -> 276 us
  blocking collectives: 46 us -> 98.7 us
  local copies, waits for them, and re-layouts: 91.1 us -> 141 us
  other arithmetic: 17.6 us -> 34.5 us
  starting transfers between devices: 0.2 us -> 7.97 us
  matrix products: 18.9 us -> 25.4 us
    all_gather x2, waiting for transfers between devices: 127 us -> 61.4 us  [entering(): gathered = jax.tree.map(lambda a: lax.all_gather(a, axis), part)]
    all_gather x1, blocking collectives: 24.6 us -> 76.3 us  [local(): lax.all_gather(scales, 'seq', axis=0, tiled=True)]
    unnamed x6 -> x5, waiting for transfers between devices: 107 us -> 146 us
    all_gather x1 -> x0, waiting for transfers between devices: 28.6 us -> none  [local(): lax.all_gather(weight_codes, 'seq', axis=0, tiled=True)]
    convert_element_type x0 -> x2, local copies, waits for them, and re-layouts: none -> 23.8 us  [the longest x1 11.9 us: dequantize(): code_rows.astype(jnp.float32)]
    convert_element_type x1 -> x2, other arithmetic: 3.92 us -> 23.5 us  [dequantize(): return spread.reshape(row_count, col_count).astype(jnp.bfloat16)]
    unnamed x25 -> x57, local copies, waits for them, and re-layouts: 17 us -> 33.5 us
    mul x0 -> x2, local copies, waits for them, and re-layouts: none -> 16.5 us  [dequantize(): spread = spread * scale_rows.astype(jnp.float32)[:, :, None]]
  transfers between devices with their start and end apart: 5 -> 5, of which waited for: 5 -> 4; matrix products, arithmetic and copies ran while one was open for 3% -> 18% of each run, Pallas kernels for 0% -> 0%
where the time goes in v1:
time: 604 us; the launch traced here: 600 us
  waiting for transfers between devices  276 us (46%)
  local copies, waits for them, and re-layouts  141 us (23%)
  blocking collectives  98.7 us (16%)
  other arithmetic  34.5 us (6%)
  matrix products  25.4 us (4%)
  between operations  14.2 us (2%)
  starting transfers between devices  7.97 us (1%)
    unnamed x5, waiting for transfers between devices  146 us
    all_gather x1, blocking collectives, local(): lax.all_gather(scales, 'seq', axis=0, tiled=True)  76.3 us
    psum x1, waiting for transfers between devices, local(): summed_grad = lax.psum(partial_grad, 'dp')  68.7 us
    all_gather x2, waiting for transfers between devices, entering(): gathered = jax.tree.map(lambda a: lax.all_gather(a, axis), part)  61.4 us
    dynamic_slice x62, local copies, waits for them, and re-layouts, one(): lax.dynamic_index_in_dim(a, source, 0, False)  44.4 us
    unnamed x57, local copies, waits for them, and re-layouts  33.5 us
    convert_element_type x2, other arithmetic, dequantize(): return spread.reshape(row_count, col_count).astype(jnp.bfloat16)  23.5 us
    all_gather x1, blocking collectives, entering(): gathered = jax.tree.map(lambda a: lax.all_gather(a, axis), part)  22.3 us
  transfers between devices with their start and end apart: 5, of which 4 were waited for; matrix products, arithmetic and copies ran while one was open for 18% of the time, Pallas kernels for 0%

profile of v1, /device:TPU:2, one launch (start us, length us, event | category | flops | bytes accessed | tf_op | source)
XLA Modules:
  0.0 599.9 jit_solution(6400618546236057267)
XLA Ops:
  22.5 2.3 copy-done.4
  24.8 7.8 %all-to-all-start = ((bf16[32,64,1280]{2,1,0:T(8,128)(2,1)}), bf16[32,64,1280]{2,1,0:T(8,128)(2,1)}, u32[]{:S(2)}, u32[]{:S(2)}) async-start(bf16[32,64,1280]{2,1,0:T(8,128)(2,1)} %bitcast.137), calls=%async_computation | async-start | bytes 10485760 | tf_op jit(solution)/shard_map/all_to_all | solution.py:10
  33.4 76.3 %all-gather.1 = bf16[32,64,10]{1,2,0:T(8,128)(2,1)S(1)} all-gather(bf16[1,64,10]{1,2,0:T(8,128)(2,1)S(1)} %bitcast.152), channel_id=1, replica_groups=mesh['dp'=8,'seq'=32] {'seq'}, dimensions={0}, use_global_device_ids=true | all-gather | bytes 42240 | tf_op jit(solution)/shard_map/all_gather | solution.py:114
  112.1 11.9 %reshape.198 = f32[2048,10,128]{2,1,0:T(8,128)} reshape(bf16[32,64,1280]{2,1,0:T(8,128)(2,1)} %all-to-all-done) | data formatting | bytes 15728640 | tf_op jit(solution)/shard_map/convert_element_type | solution.py:32
  124.0 14.6 %multiply_convert_fusion = bf16[2048,10,128]{2,1,0:T(8,128)(2,1)} fusion(f32[2048,10,128]{2,1,0:T(8,128)} %reshape.198, f32[2048,10]{1,0:T(8,128)S(1)} %bitcast.135), kind=kLoop, calls=%fused_computation.6 | loop fusion | flops 5242880 | bytes 15810560 | tf_op jit(solution)/shard_map/convert_element_type | solution.py:34
  138.6 11.9 %copy.88 = bf16[2048,10,128]{0,2,1:T(8,128)(2,1)} copy(bf16[2048,10,128]{2,1,0:T(8,128)(2,1)} %multiply_convert_fusion) | data formatting | bytes 10485760 | tf_op jit(solution)/shard_map/convert_element_type | solution.py:34
  150.5 4.0 fusion.1
  157.5 22.3 %all-gather = f32[32,16,1]{1,2,0:T(1,128)} all-gather(f32[1,16,1]{1,2,0:T(1,128)S(1)} %exp.58), channel_id=2, replica_groups=mesh['dp'=8,'seq'=32] {'seq'}, dimensions={0}, use_global_device_ids=true | all-gather | bytes 2112 | tf_op jit(solution)/shard_map/all_gather | solution.py:17
  181.7 54.0 %all-gather.5.cloned.1.call-done = f32[32,16,128,64]{2,3,1,0:T(8,128)} async-done(((f32[1,16,128,64]{2,3,1,0:T(8,128)}), f32[32,16,128,64]{2,3,1,0:T(8,128)}) %all-gather.5.cloned.1.call-update) | async-done | bytes 16777232 | tf_op jit(solution)/shard_map/all_gather | solution.py:17
  235.8 69.3 %while.16 = (s32[]{:T(128)}, f32[16,128,64]{2,1,0:T(8,128)S(1)}, s32[]{:T(128)}, f32[32,16]{1,0:T(8,128)}, f32[32,16,128,64]{2,3,1,0:T(8,128)}, /*index=5*/s32[]{:T(128)}, s32[]{:T(128)}, s32[]{:T(128)}, s32[]{:T(128)}) while((s32[]{:T(128)}, f32[16,128,64]{2,1,0:T(8,128)S(1)}, s32[]{:T(128)}, f32[32,16]{1,0:T(8,128)}, ...), condition=%wide.region_2.3_spmd, body=%wide.region_1.2_spmd.sunk | while | flops 262150 | bytes 3670355 | solution.py:26
  276.2 1.2 constant_dynamic-slice_fusion.4
  306.1 1.9 convolution_bitcast_fusion.7
  307.9 7.4 %all-gather.7.cloned.1.call-done = f32[32,16,128,64]{2,3,1,0:T(8,128)} async-done(((f32[1,16,128,64]{2,3,1,0:T(8,128)}), f32[32,16,128,64]{2,3,1,0:T(8,128)}) %all-gather.7.cloned.1.call-update) | async-done | bytes 16777232 | tf_op jit(solution)/shard_map/all_gather | solution.py:17
  315.5 4.9 while.17
  323.9 1.6 fusion.10
  325.5 5.3 convolution_bitcast_fusion
  330.8 11.3 %copy.120 = f32[2048,1280]{1,0:T(8,128)} copy(f32[2048,1280]{0,1:T(8,128)} %convolution_bitcast_fusion) | data formatting | bytes 20971520
  343.7 5.3 mul.263.clone
  349.0 11.2 %copy.106 = f32[2048,1280]{1,0:T(8,128)} copy(f32[2048,1280]{0,1:T(8,128)} %bitcast.134) | data formatting | bytes 20971520 | tf_op jit(solution)/shard_map/mul | solution.py:33
  360.2 8.9 %fusion = bf16[2048,1280]{1,0:T(8,128)(2,1)} fusion(f32[2048,1280]{1,0:T(8,128)} %copy.106, bf16[32,64,1280]{2,1,0:T(8,128)(2,1)} %all-to-all-done), kind=kLoop, calls=%fused_computation.8 | loop fusion | flops 7864320 | bytes 20971520 | tf_op jit(solution)/shard_map/convert_element_type | solution.py:34
  369.1 146.1 %reduce-scatter.4.cloned.1.call-done = f32[64,1280]{1,0:T(8,128)} async-done(((f32[2048,1280]{1,0:T(8,128)}), f32[64,1280]{1,0:T(8,128)}) %reduce-scatter.4.cloned.1.call-update) | async-done | bytes 327696
  515.2 2.1 copy.121
  517.3 5.3 convolution_bitcast_fusion.1
  522.6 68.7 %all-reduce.2.cloned.1.call-done = f32[64,1280]{0,1:T(8,128)} async-done(((f32[64,1280]{0,1:T(8,128)}), f32[64,1280]{0,1:T(8,128)}) %all-reduce.2.cloned.1.call-update) | async-done | bytes 327696 | tf_op jit(solution)/shard_map/psum | solution.py:165
  (214 shorter events, 102.6 us)
Async XLA Ops:
  7.2 143.3 %copy-start = (bf16[1,128,2048]{2,1,0:T(8,128)(2,1)S(1)}, bf16[1,128,2048]{2,1,0:T(8,128)(2,1)}, u32[]{:S(2)}) copy-start(bf16[1,128,2048]{2,1,0:T(8,128)(2,1)} %param.9) | copy-start | bytes 1572868
  7.2 15.0 %copy-start.1 = (bf16[64,1280]{1,0:T(8,128)(2,1)S(1)}, bf16[64,1280]{1,0:T(8,128)(2,1)}, u32[]{:S(2)}) copy-start(bf16[64,1280]{1,0:T(8,128)(2,1)} %param.10) | copy-start | bytes 491524
  22.5 2.3 copy-start.4
  24.8 7.9 %copy-start.7 = (f32[1,16,128]{2,1,0:T(8,128)S(1)}, f32[1,16,128]{2,1,0:T(8,128)}, u32[]{:S(2)}) copy-start(f32[1,16,128]{2,1,0:T(8,128)} %param.12) | copy-start | bytes 24580
  24.8 8.3 %copy-start.6 = (bf16[1,128,1024]{2,1,0:T(8,128)(2,1)S(1)}, bf16[1,128,1024]{2,1,0:T(8,128)(2,1)}, u32[]{:S(2)}) copy-start(bf16[1,128,1024]{2,1,0:T(8,128)(2,1)} %param.13) | copy-start | bytes 786436
  24.8 8.5 %copy-start.9 = (bf16[64,10]{0,1:T(8,128)(2,1)S(1)}, bf16[64,10]{0,1:T(8,128)(2,1)}, u32[]{:S(2)}) copy-start(bf16[64,10]{0,1:T(8,128)(2,1)} %param.11) | copy-start | bytes 3844
  24.8 87.2 %all-to-all-start = ((bf16[32,64,1280]{2,1,0:T(8,128)(2,1)}), bf16[32,64,1280]{2,1,0:T(8,128)(2,1)}, u32[]{:S(2)}, u32[]{:S(2)}) async-start(bf16[32,64,1280]{2,1,0:T(8,128)(2,1)} %bitcast.137), calls=%async_computation | async-start | bytes 10485760 | tf_op jit(solution)/shard_map/all_to_all | solution.py:10
  32.6 203.1 %all-gather.5.cloned.1.call-start = ((), (), s32[]{:S(2)}) async-start(), calls=%async_computation.2 | async-start | bytes 17301504 | tf_op jit(solution)/shard_map/all_gather | solution.py:17
  33.3 146.6 %copy-start.5 = (bf16[1,128,1024]{1,2,0:T(8,128)(2,1)}, bf16[1,128,1024]{1,2,0:T(8,128)(2,1)S(1)}, u32[]{:S(2)}) copy-start(bf16[1,128,1024]{1,2,0:T(8,128)(2,1)S(1)} %copy.91) | copy-start | bytes 786436
  110.1 13.9 %copy-start.2 = (f32[32,64,10]{2,1,0:T(8,128)}, f32[32,64,10]{2,1,0:T(8,128)S(1)}, u32[]{:S(2)}) copy-start(f32[32,64,10]{2,1,0:T(8,128)S(1)} %copy.115) | copy-start | bytes 245764
  155.6 159.8 %all-gather.7.cloned.1.call-start = ((), (), s32[]{:S(2)}) async-start(), calls=%async_computation.3 | async-start | bytes 17301504 | tf_op jit(solution)/shard_map/all_gather | solution.py:17
  157.5 357.8 %reduce-scatter.4.cloned.1.call-start = ((), (), s32[]{:S(2)}) async-start(), calls=%async_computation.5 | async-start | bytes 10813440
  179.9 55.9 %copy-start.8 = (pred[128,128]{0,1:T(8,128)(4,1)}, pred[128,128]{0,1:T(8,128)(4,1)S(1)}, u32[]{:S(2)}) copy-start(pred[128,128]{0,1:T(8,128)(4,1)S(1)} %iota_compare_fusion) | copy-start | bytes 49156
  342.1 1.2 copy-start.3
  342.2 249.1 %all-reduce.2.cloned.1.call-start = ((), (), s32[]{:S(2)}) async-start(), calls=%async_computation.4 | async-start | bytes 1310720 | tf_op jit(solution)/shard_map/psum | solution.py:165
Sparse Core Ops, SparseCore 0:
  155.7 79.9 all-gather.4
  238.3 77.0 all-gather.6
  342.3 172.9 reduce-scatter.3
  517.6 73.7 all-reduce.1
